TPU v7x, 512 devices: a whole 4x8x8 slice. The times are simulated.
512 devices in a mesh: dp: 4 (over z_lo, core), ctx: 128 (over x, y, z_hi).
Axes of the slice: x: 4, y: 8, z: 8 (z_hi: 4, z_lo: 2; z = z_hi * 2 + z_lo), core: 2. Of those that a mesh axis runs over, the one named last changes fastest.
Arguments:
- query: bfloat16 [4, 32768, 1024], P('dp', 'ctx'), may hold values from -150 to 150
- key: bfloat16 [4, 32768, 1024], P('dp', 'ctx'), may hold values from -3 to 3
- value: bfloat16 [4, 32768, 1024], P('dp', 'ctx'), may hold values from -6 to 6
- grad_out: bfloat16 [4, 32768, 1024], P('dp', 'ctx'), may hold values from -30 to 30
- clause: int32 [4, 32768], P('dp', 'ctx'), may hold values from 0 to 2047, never falling along the last dimension, each value on 1 to 48 neighbouring positions
- bias_table: float32 [32, 2], replicated, may hold values from -1.5 to 1.5
Outputs:
- attended: bfloat16 [4, 32768, 1024], P('dp', 'ctx')
- query_gradient: bfloat16 [4, 32768, 1024], P('dp', 'ctx')
- key_gradient: bfloat16 [4, 32768, 1024], P('dp', 'ctx')
- value_gradient: bfloat16 [4, 32768, 1024], P('dp', 'ctx')
- bias_grad: float32 [32, 2], replicated
Inputs may be any that keep to these rules, and one draw needn't show every extreme that they name: Clause ids never fall along a document; a clause holds 1 to 48 tokens, and some clause holds exactly 48.
All inputs are finite; a program needn't handle non-finite values.
Results may differ from a plain program's by a relative error of at most 0.009.
Values may be sent and summed in bfloat16 or wider, within the bound.
No kernel may reach another device: no remote copies, remote signals or barrier semaphores. Data moves between devices by JAX's collectives and lax.ppermute only.
A program may use at most 128 MiB of HBM per device.

v0:
```python
import jax
import jax.numpy as jnp
from jax import lax
from jax.sharding import PartitionSpec as P

HEADS = 8
WINDOW = 512
BUCKETS = 32
DILATION_FIRST = 1
DILATION_SECOND = 8
DILATION_THIRD = 32


def swapped(block, axis, bit):
    count = lax.axis_size(axis)
    route = []
    for low in range(count):
        high = low | 1 << bit
        if high != low and high < count:
            route += [(low, high), (high, low)]
    return lax.ppermute(block, axis, route)


def shifted(value, axis, steps):
    count = lax.axis_size(axis)
    leading, last = (max(0, -steps), min(count, count - steps))
    return lax.ppermute(value, axis, [(source, source + steps) for source in range(leading, last)])


def with_halo(shard, sides, width):
    for axis, dim in sides:
        size, length = (lax.axis_size(axis), shard.shape[dim])
        up = [(i, (i + 1) % size) for i in range(size - 1)]
        down = [(j, i) for i, j in up]
        last = lax.slice_in_dim(shard, length - width, length, axis=dim)
        leading = lax.slice_in_dim(shard, 0, width, axis=dim)
        before = lax.ppermute(last, axis, up)
        after = lax.ppermute(leading, axis, down)
        shard = jnp.concatenate([before, shard, after], axis=dim)
    return shard


def sample_rows(matrix, initial_flag, dilation_rate):
    count = matrix.shape[0] // dilation_rate
    head_dim = matrix.shape[1] // HEADS
    grid = matrix.reshape(count, dilation_rate, HEADS, head_dim)
    return jnp.concatenate(
        [grid[:, 0, initial_flag], grid[:, dilation_rate // 2, initial_flag + 1]], axis=1
    )


def spread_rows(sampled, dilation_rate):
    count = sampled.shape[0]
    grid = jnp.zeros((count, dilation_rate) + sampled.shape[1:], sampled.dtype)
    grid = grid.at[:, 0, 0].set(sampled[:, 0]).at[:, dilation_rate // 2, 1].set(sampled[:, 1])
    return grid.reshape((count * dilation_rate,) + sampled.shape[1:])


def upper_half(bit):
    index = lax.axis_index("ctx")
    return index // 2**bit % 2 == 1


def double_rows(block, bits):
    for bit in range(bits):
        other = swapped(block, "ctx", bit)
        block = jnp.where(
            upper_half(bit),
            jnp.concatenate([other, block], axis=0),
            jnp.concatenate([block, other], axis=0),
        )
    return block


def halve_sums(block, bits):
    for bit in reversed(range(bits)):
        half = block.shape[0] // 2
        lower, higher = (block[:half], block[half:])
        upper = upper_half(bit)
        outgoing = jnp.where(upper, lower, higher)
        staying = jnp.where(upper, higher, lower)
        block = staying + swapped(outgoing.astype(jnp.bfloat16), "ctx", bit).astype(outgoing.dtype)
    return block


def span_rows(block, bits):
    return double_rows(block, bits)


def span_sums(block, bits):
    return halve_sums(block, bits)


def rows_side(score_matrix, every_key_rows, every_value_rows, gradient_list, score_scale):
    top = jnp.max(score_matrix, axis=-1, keepdims=True)
    raised = jnp.exp(score_matrix - top)
    totals = jnp.sum(raised, axis=-1, keepdims=True)
    shares = raised / totals
    softmax_weights = shares.astype(jnp.bfloat16)
    attended = jnp.einsum(
        "ezb,beo->zeo", softmax_weights, every_value_rows, preferred_element_type=jnp.float32
    )
    weight_gradient = jnp.einsum(
        "wvx,yvx->vwy", gradient_list, every_value_rows, preferred_element_type=jnp.float32
    )
    delta = jnp.sum(shares * weight_gradient, axis=-1, keepdims=True)
    logit_grads = shares * (weight_gradient - delta)
    score_gradient = logit_grads.astype(jnp.bfloat16)
    query_gradient = (
        jnp.einsum(
            "ezb,beo->zeo", score_gradient, every_key_rows, preferred_element_type=jnp.float32
        )
        * score_scale
    )
    return (
        attended,
        query_gradient,
        softmax_weights,
        score_gradient,
        logit_grads,
        top,
        totals,
        delta,
    )


def keys_side(softmax_weights, score_gradient, query_matrix, gradient_list, score_scale):
    key_gradient = (
        jnp.einsum("vjb,jvw->bvw", score_gradient, query_matrix, preferred_element_type=jnp.float32)
        * score_scale
    )
    value_gradient = jnp.einsum(
        "vjb,jvw->bvw", softmax_weights, gradient_list, preferred_element_type=jnp.float32
    )
    return (key_gradient, value_gradient)


def bucket_lookup(bucket, table):
    running = jnp.zeros((table.shape[1],) + bucket.shape, jnp.float32)
    for level in range(BUCKETS):
        running = jnp.where(bucket[None] == level, table[level][:, None, None], running)
    return running


def bucket_sums(bucket, logit_grads):
    totals = [
        jnp.sum(jnp.where(bucket[None] == level, logit_grads, 0.0), axis=(1, 2))
        for level in range(BUCKETS)
    ]
    return jnp.stack(totals, axis=0)


def pass_rim(rim, offset):
    return shifted(rim.astype(jnp.bfloat16), "ctx", offset).astype(rim.dtype)


def band_part(query_rows, key_rows, value_rows, grad_rows, clause_rows, table, score_scale):
    rows, width = query_rows.shape
    head_dim = width // HEADS
    wide = 2 * head_dim
    half = WINDOW // 2
    pair_rows = jnp.concatenate([key_rows[:, :wide], value_rows[:, :wide]], axis=1)
    extended, extended_clause = (
        with_halo(pair_rows, (("ctx", 0),), half),
        with_halo(clause_rows, (("ctx", 0),), half),
    )
    reach = rows + 2 * half
    nearby_key_rows = extended[:, :wide].reshape(reach, 2, head_dim)
    values_near = extended[:, wide:].reshape(reach, 2, head_dim)
    query_matrix = query_rows[:, :wide].reshape(rows, 2, head_dim)
    gradient_list = grad_rows[:, :wide].reshape(rows, 2, head_dim)
    start = lax.axis_index("ctx") * rows
    length = rows * lax.axis_size("ctx")
    local_query = jnp.arange(rows)[:, None]
    local_key = jnp.arange(reach)[None, :] - half
    global_key = start + local_key
    allowed = (jnp.abs(local_query - local_key) < half) & (global_key >= 0) & (global_key < length)
    bucket = jnp.minimum(jnp.abs(clause_rows[:, None] - extended_clause[None, :]), BUCKETS - 1)
    score_matrix = (
        jnp.einsum(
            "wvx,yvx->vwy", query_matrix, nearby_key_rows, preferred_element_type=jnp.float32
        )
        * score_scale
    )
    score_matrix = jnp.where(allowed[None], score_matrix + bucket_lookup(bucket, table), -jnp.inf)
    attended, query_gradient, softmax_weights, score_gradient, logit_grads, top, totals, delta = (
        rows_side(score_matrix, nearby_key_rows, values_near, gradient_list, score_scale)
    )
    key_gradient, value_gradient = keys_side(
        softmax_weights, score_gradient, query_matrix, gradient_list, score_scale
    )
    sums = jnp.concatenate(
        [key_gradient.reshape(reach, wide), value_gradient.reshape(reach, wide)], axis=1
    )
    own = sums[half : half + rows]
    from_next = pass_rim(sums[:half], -1)
    from_prev = pass_rim(sums[half + rows :], 1)
    own = own.at[rows - half :].add(from_next).at[:half].add(from_prev)
    own_key = own[:, :wide].reshape(rows, 2, head_dim)
    own_value = own[:, wide:].reshape(rows, 2, head_dim)
    return (attended, query_gradient, own_key, own_value, bucket_sums(bucket, logit_grads))


def dilated(
    query_rows, key_rows, value_rows, grad_rows, initial_flag, dilation_rate, bits, score_scale
):
    head_dim = query_rows.shape[1] // HEADS
    wide = 2 * head_dim
    picked_query = sample_rows(query_rows, initial_flag, dilation_rate)
    picked_key = sample_rows(key_rows, initial_flag, dilation_rate)
    picked_value = sample_rows(value_rows, initial_flag, dilation_rate)
    picked_grad = sample_rows(grad_rows, initial_flag, dilation_rate)
    count = picked_query.shape[0]
    gathered = span_rows(jnp.concatenate([picked_key, picked_value], axis=1), bits)
    gathered_rows = gathered.shape[0]
    every_key_rows = gathered[:, :wide].reshape(gathered_rows, 2, head_dim)
    every_value_rows = gathered[:, wide:].reshape(gathered_rows, 2, head_dim)
    query_matrix = picked_query.reshape(count, 2, head_dim)
    gradient_list = picked_grad.reshape(count, 2, head_dim)
    score_matrix = (
        jnp.einsum("wvx,yvx->vwy", query_matrix, every_key_rows, preferred_element_type=jnp.float32)
        * score_scale
    )
    attended, query_gradient, softmax_weights, score_gradient, logit_grads, top, totals, delta = (
        rows_side(score_matrix, every_key_rows, every_value_rows, gradient_list, score_scale)
    )
    key_gradient, value_gradient = keys_side(
        softmax_weights, score_gradient, query_matrix, gradient_list, score_scale
    )
    partial_sums = jnp.concatenate(
        [key_gradient.reshape(gathered_rows, wide), value_gradient.reshape(gathered_rows, wide)],
        axis=1,
    )
    own = span_sums(partial_sums, bits)
    own_key = own[:, :wide].reshape(count, 2, head_dim)
    own_value = own[:, wide:].reshape(count, 2, head_dim)
    return (
        spread_rows(attended, dilation_rate),
        spread_rows(query_gradient, dilation_rate),
        spread_rows(own_key, dilation_rate),
        spread_rows(own_value, dilation_rate),
    )


def shards(query, key, value, grad_out, clause, bias_table):
    query_rows = query[0]
    key_rows = key[0]
    value_rows = value[0]
    grad_rows = grad_out[0]
    clause_rows = clause[0]
    rows, width = query_rows.shape
    head_dim = width // HEADS
    score_scale = head_dim ** (-0.5)
    bucket_bit_count = lax.axis_size("ctx").bit_length() - 1
    band = band_part(
        query_rows, key_rows, value_rows, grad_rows, clause_rows, bias_table, score_scale
    )
    pieces = [band[:4]]
    for initial_flag, dilation_rate, bits in (
        (2, DILATION_FIRST, max(bucket_bit_count - 5, 1)),
        (4, DILATION_SECOND, bucket_bit_count - 2),
        (6, DILATION_THIRD, bucket_bit_count),
    ):
        pieces.append(
            dilated(
                query_rows,
                key_rows,
                value_rows,
                grad_rows,
                initial_flag,
                dilation_rate,
                bits,
                score_scale,
            )
        )
    bias_grad = lax.psum(band[4], ("dp", "ctx"))
    joined = [
        jnp.concatenate([piece[slot] for piece in pieces], axis=1)
        .reshape(1, rows, width)
        .astype(jnp.bfloat16)
        for slot in range(4)
    ]
    return (joined[0], joined[1], joined[2], joined[3], bias_grad)


def solution(mesh):
    in_specs = (
        P("dp", "ctx", None),
        P("dp", "ctx", None),
        P("dp", "ctx", None),
        P("dp", "ctx", None),
        P("dp", "ctx"),
        P(),
    )
    out_specs = (
        P("dp", "ctx", None),
        P("dp", "ctx", None),
        P("dp", "ctx", None),
        P("dp", "ctx", None),
        P(),
    )
    return jax.shard_map(shards, mesh=mesh, in_specs=in_specs, out_specs=out_specs, check_vma=False)
```

profile of v0, /device:TPU:6, one launch (start us, length us, event | category | flops | bytes accessed | tf_op | source)
XLA Modules:
  0.0 409.0 jit_solution(8975889016358861328)
XLA Ops:
  0.6 14.2 %collective-permute-start.3 = (s32[256]{0:T(256)}, s32[256]{0:T(256)}, u32[]{:S(2)}, u32[]{:S(2)}) collective-permute-start(s32[256]{0:T(256)} %bitcast.409), channel_id=1, source_target_pairs={{1,0},{2,1},{3,2},{4,3},{5,4},{6,5},{7,6},{8,7},{9,8},{10,9},{11,1... | collective-permute-start | bytes 3080 | tf_op jit(solution)/shard_map/ppermute | solution.py:38
  14.9 1.9 collective-permute-start.2
  19.1 9.0 %collective-permute-start.1 = (bf16[256,512]{0,1:T(8,128)(2,1)}, bf16[256,512]{0,1:T(8,128)(2,1)}, u32[]{:S(2)}, u32[]{:S(2)}) collective-permute-start(bf16[256,512]{0,1:T(8,128)(2,1)} %pad_maximum_fusion.9), channel_id=1, source_target_pairs={{1,0},{2,1},{3,2},{4,3},{5,4},{6,5},{7,6},{8,7},{9,8},{10,9},{11,1... | collective-permute-start | bytes 786440 | tf_op jit(solution)/shard_map/ppermute | solution.py:38
  46.3 4.8 %collective-permute-start.6 = (bf16[32,512]{1,0:T(8,128)(2,1)S(1)}, bf16[32,512]{1,0:T(8,128)(2,1)S(1)}, u32[]{:S(2)}, u32[]{:S(2)}) collective-permute-start(bf16[32,512]{1,0:T(8,128)(2,1)S(1)} %pad_maximum_fusion.21), channel_id=1, source_target_pairs={{0,1},{1,0},{2,3},{3,2},{4,5},{5,4},{6,7},{7,6},{8,9},{9,8},{10,11... | collective-permute-start | bytes 98312 | tf_op jit(solution)/shard_map/ppermute | solution.py:21
  53.8 4.0 collective-permute-start.12
  58.5 5.1 %collective-permute-done.12 = bf16[16,512]{1,0:T(8,128)(2,1)S(1)} collective-permute-done((bf16[16,512]{1,0:T(8,128)(2,1)S(1)}, bf16[16,512]{1,0:T(8,128)(2,1)S(1)}, u32[]{:S(2)}, u32[]{:S(2)}) %collective-permute-start.12) | collective-permute-done | bytes 16416 | tf_op jit(solution)/shard_map/ppermute | solution.py:21
  65.6 5.4 %collective-permute-start.7 = (bf16[64,512]{1,0:T(8,128)(2,1)S(1)}, bf16[64,512]{1,0:T(8,128)(2,1)S(1)}, u32[]{:S(2)}, u32[]{:S(2)}) collective-permute-start(bf16[64,512]{1,0:T(8,128)(2,1)S(1)} %maximum_select_fusion.10), channel_id=1, source_target_pairs={{0,2},{2,0},{1,3},{3,1},{4,6},{6,4},{5,7},{7,5},{8,10},{10,8},{9,1... | collective-permute-start | bytes 196616 | tf_op jit(solution)/shard_map/ppermute | solution.py:21
  71.1 6.8 %collective-permute-start.14 = (bf16[64,512]{1,0:T(8,128)(2,1)S(1)}, bf16[64,512]{1,0:T(8,128)(2,1)S(1)}, u32[]{:S(2)}, u32[]{:S(2)}) collective-permute-start(bf16[64,512]{1,0:T(8,128)(2,1)S(1)} %maximum_select_fusion.11), channel_id=1, source_target_pairs={{0,8},{8,0},{1,9},{9,1},{2,10},{10,2},{3,11},{11,3},{4,12},{12,4},... | collective-permute-start | bytes 196616 | tf_op jit(solution)/shard_map/ppermute | solution.py:21
  80.6 4.3 %collective-permute-start.15 = (bf16[128,512]{1,0:T(8,128)(2,1)S(1)}, bf16[128,512]{1,0:T(8,128)(2,1)S(1)}, u32[]{:S(2)}, u32[]{:S(2)}) collective-permute-start(bf16[128,512]{1,0:T(8,128)(2,1)S(1)} %maximum_select_fusion.9), channel_id=1, source_target_pairs={{0,16},{16,0},{1,17},{17,1},{2,18},{18,2},{3,19},{19,3},{4,20},{20... | collective-permute-start | bytes 393224 | tf_op jit(solution)/shard_map/ppermute | solution.py:21
  84.9 4.9 %fusion.56 = (pred[256,768]{0,1:T(8,128)(4,1)S(1)}, pred[256,768]{0,1:T(8,128)(4,1)S(1)}, pred[256,768]{0,1:T(8,128)(4,1)S(1)}, pred[256,768]{0,1:T(8,128)(4,1)S...) fusion(s32[768]{0:T(1024)S(1)} %pad_add_fusion, ...), kind=kLoop, calls=%fused_computation.134 | loop fusion | flops 6881280 | bytes 6295552 | tf_op jit(solution)/shard_map/eq | solution.py:141
  90.2 3.0 collective-permute-start.9
  93.6 7.5 %collective-permute-start.16 = (bf16[256,512]{1,0:T(8,128)(2,1)S(1)}, bf16[256,512]{1,0:T(8,128)(2,1)}, u32[]{:S(2)}, u32[]{:S(2)}) collective-permute-start(bf16[256,512]{1,0:T(8,128)(2,1)S(1)} %maximum_select_fusion.7), channel_id=1, source_target_pairs={{0,32},{32,0},{1,33},{33,1},{2,34},{34,2},{3,35},{35,3},{4,36},{36... | collective-permute-start | bytes 786440 | tf_op jit(solution)/shard_map/ppermute | solution.py:21
  103.5 5.7 %fusion.9 = f32[2,256,768]{1,2,0:T(8,128)S(1)} fusion(bf16[768,2,128]{0,2,1:T(8,128)(2,1)S(1)} %bitcast.347, bf16[256,2,128]{0,2,1:T(8,128)(2,1)S(1)} %bitcast.361, f32[2]{0:T(128)S(1)} %copy-done.182, f32[2]{0:T(128)S(1)} %copy-done.183, f32[2]{0:T(128)S(1)} %copy-done.121, f32[2]{0:T(128)S(1)} %copy-done.122, f32[2]{0:T(128)S(1)} %copy-done.123, ...), kind=kOutput, calls=%fused_computation.25 | convolution fusion | flops 114425856 | bytes 8585472 | tf_op jit(solution)/shard_map/wvx,yvx->vwy/dot_general | solution.py:180
  110.9 2.5 fusion.68
  115.8 5.5 %select_reduce_fusion = (f32[2]{0:T(128)}, f32[2]{0:T(128)}, f32[2]{0:T(128)}, f32[2]{0:T(128)}, f32[2]{0:T(128)}, /*index=5*/f32[2]{0:T(128)}, f32[2]{0:T(128)}...) fusion(pred[256,768]{0,1:T(8,128)(4,1)S(1)} %copy-done.39, ...), kind=kLoop, calls=%fused_computation.26 | loop fusion | flops 15335388 | bytes 8261776 | tf_op jit(solution)/shard_map/reduce_sum | solution.py:147
  121.4 4.4 %select_reduce_fusion.18 = (f32[2]{0:T(128)}, f32[2]{0:T(128)}, f32[2]{0:T(128)}, f32[2]{0:T(128)}, f32[2]{0:T(128)}, /*index=5*/f32[2]{0:T(128)}, f32[2]{0:T(12...) fusion(f32[2,256,768]{1,2,0:T(8,128)S(1)} %get-tuple-element.442, ...), kind=kLoop, calls=%fused_computation.44 | loop fusion | flops 11010020 | bytes 4325488 | tf_op jit(solution)/shard_map/reduce_sum | solution.py:147
  128.5 3.1 fusion.15
  131.5 5.1 %collective-permute-start.18 = (bf16[256,512]{0,1:T(8,128)(2,1)}, bf16[256,512]{0,1:T(8,128)(2,1)}, u32[]{:S(2)}, u32[]{:S(2)}) collective-permute-start(bf16[256,512]{0,1:T(8,128)(2,1)} %get-tuple-element.449), channel_id=1, source_target_pairs={{1,0},{2,1},{3,2},{4,3},{5,4},{6,5},{7,6},{8,7},{9,8},{10,9},{11,1... | collective-permute-start | bytes 786440 | tf_op jit(solution)/shard_map/ppermute | solution.py:27
  139.7 4.6 %collective-permute-start.5 = (bf16[512,512]{0,1:T(8,128)(2,1)S(1)}, bf16[512,512]{0,1:T(8,128)(2,1)}, u32[]{:S(2)}, u32[]{:S(2)}) collective-permute-start(bf16[512,512]{0,1:T(8,128)(2,1)S(1)} %maximum_select_fusion.3), channel_id=1, source_target_pairs={{0,2},{2,0},{1,3},{3,1},{4,6},{6,4},{5,7},{7,5},{8,10},{10,8},{9,1... | collective-permute-start | bytes 1572872 | tf_op jit(solution)/shard_map/ppermute | solution.py:21
  147.5 111.7 %psum.7 = f32[32,2]{0,1:T(2,128)} all-reduce(f32[32,2]{0,1:T(2,128)S(1)} %stack.131), channel_id=1, replica_groups=mesh['dp'=4,'ctx'=128] {'dp','ctx'}, use_global_device_ids=true, to_apply=%region_44.45 | all-reduce | flops 64 | bytes 512 | tf_op jit(solution)/shard_map/psum | solution.py:276
  260.3 4.0 collective-permute-start.10
  264.3 2.0 maximum_select_fusion.5
  266.3 4.6 %collective-permute-start.17 = (bf16[512,512]{1,0:T(8,128)(2,1)}, bf16[512,512]{1,0:T(8,128)(2,1)}, u32[]{:S(2)}, u32[]{:S(2)}) collective-permute-start(bf16[512,512]{1,0:T(8,128)(2,1)} %maximum_select_fusion.5), channel_id=1, source_target_pairs={{0,64},{64,0},{1,65},{65,1},{2,66},{66,2},{3,67},{67,3},{4,68},{68... | collective-permute-start | bytes 1572872 | tf_op jit(solution)/shard_map/ppermute | solution.py:21
  275.1 2.1 fusion.133
  279.9 2.5 multiply_reduce_fusion
  284.7 4.5 %collective-permute-start.20 = (bf16[512,512]{0,1:T(8,128)(2,1)}, bf16[512,512]{0,1:T(8,128)(2,1)}, u32[]{:S(2)}, u32[]{:S(2)}) collective-permute-start(bf16[512,512]{0,1:T(8,128)(2,1)} %select_convert_fusion.2), channel_id=1, source_target_pairs={{0,2},{2,0},{1,3},{3,1},{4,6},{6,4},{5,7},{7,5},{8,10},{10,8},{9,1... | collective-permute-start | bytes 1572872 | tf_op jit(solution)/shard_map/ppermute | solution.py:21
  302.2 4.3 %collective-permute-start.22 = (bf16[512,512]{1,0:T(8,128)(2,1)}, bf16[512,512]{1,0:T(8,128)(2,1)}, u32[]{:S(2)}, u32[]{:S(2)}) collective-permute-start(bf16[512,512]{1,0:T(8,128)(2,1)} %select_convert_fusion.1), channel_id=1, source_target_pairs={{0,16},{16,0},{1,17},{17,1},{2,18},{18,2},{3,19},{19,3},{4,20},{20... | collective-permute-start | bytes 1572872 | tf_op jit(solution)/shard_map/ppermute | solution.py:21
  309.4 2.0 copy.639
  313.0 2.0 copy.636
  320.9 2.5 copy.675
  324.8 2.6 copy.674
  327.4 2.5 select_convert_fusion
  329.9 4.6 %collective-permute-start.27 = (bf16[512,512]{1,0:T(8,128)(2,1)}, bf16[512,512]{1,0:T(8,128)(2,1)}, u32[]{:S(2)}, u32[]{:S(2)}) collective-permute-start(bf16[512,512]{1,0:T(8,128)(2,1)} %select_convert_fusion), channel_id=1, source_target_pairs={{0,64},{64,0},{1,65},{65,1},{2,66},{66,2},{3,67},{67,3},{4,68},{68... | collective-permute-start | bytes 1572872 | tf_op jit(solution)/shard_map/ppermute | solution.py:21
  336.3 2.0 copy.717
  338.3 2.0 copy.718
  342.1 2.3 collective-permute-start.21
  345.7 2.2 collective-permute-start.23
  351.2 6.0 %collective-permute-done.21 = bf16[256,512]{0,1:T(8,128)(2,1)S(1)} collective-permute-done((bf16[256,512]{0,1:T(8,128)(2,1)S(1)}, bf16[256,512]{0,1:T(8,128)(2,1)S(1)}, u32[]{:S(2)}, u32[]{:S(2)}) %collective-permute-start.21) | collective-permute-done | bytes 262176 | tf_op jit(solution)/shard_map/ppermute | solution.py:21
  361.5 6.6 %collective-permute-start.29 = (bf16[128,512]{1,0:T(8,128)(2,1)S(1)}, bf16[128,512]{1,0:T(8,128)(2,1)S(1)}, u32[]{:S(2)}, u32[]{:S(2)}) collective-permute-start(bf16[128,512]{1,0:T(8,128)(2,1)S(1)} %select_convert_fusion.6), channel_id=1, source_target_pairs={{0,16},{16,0},{1,17},{17,1},{2,18},{18,2},{3,19},{19,3},{4,20},{20... | collective-permute-start | bytes 393224 | tf_op jit(solution)/shard_map/ppermute | solution.py:21
  368.2 4.5 %collective-permute-start.25 = (bf16[64,512]{1,0:T(8,128)(2,1)S(1)}, bf16[64,512]{1,0:T(8,128)(2,1)S(1)}, u32[]{:S(2)}, u32[]{:S(2)}) collective-permute-start(bf16[64,512]{1,0:T(8,128)(2,1)S(1)} %select_convert_fusion.9), channel_id=1, source_target_pairs={{0,2},{2,0},{1,3},{3,1},{4,6},{6,4},{5,7},{7,5},{8,10},{10,8},{9,1... | collective-permute-start | bytes 196616 | tf_op jit(solution)/shard_map/ppermute | solution.py:21
  372.9 6.8 %collective-permute-start.30 = (bf16[64,512]{1,0:T(8,128)(2,1)S(1)}, bf16[64,512]{1,0:T(8,128)(2,1)S(1)}, u32[]{:S(2)}, u32[]{:S(2)}) collective-permute-start(bf16[64,512]{1,0:T(8,128)(2,1)S(1)} %select_convert_fusion.8), channel_id=1, source_target_pairs={{0,8},{8,0},{1,9},{9,1},{2,10},{10,2},{3,11},{11,3},{4,12},{12,4},... | collective-permute-start | bytes 196616 | tf_op jit(solution)/shard_map/ppermute | solution.py:21
  379.7 4.5 %collective-permute-start.26 = (bf16[32,512]{1,0:T(8,128)(2,1)S(1)}, bf16[32,512]{1,0:T(8,128)(2,1)S(1)}, u32[]{:S(2)}, u32[]{:S(2)}) collective-permute-start(bf16[32,512]{1,0:T(8,128)(2,1)S(1)} %select_convert_fusion.11), channel_id=1, source_target_pairs={{0,1},{1,0},{2,3},{3,2},{4,5},{5,4},{6,7},{7,6},{8,9},{9,8},{10,11... | collective-permute-start | bytes 98312 | tf_op jit(solution)/shard_map/ppermute | solution.py:21
  384.4 3.0 collective-permute-start.31
  387.5 2.7 collective-permute-done.31
  390.2 5.2 %collective-permute-start.32 = (bf16[16,512]{1,0:T(8,128)(2,1)S(1)}, bf16[16,512]{1,0:T(8,128)(2,1)S(1)}, u32[]{:S(2)}, u32[]{:S(2)}) collective-permute-start(bf16[16,512]{1,0:T(8,128)(2,1)S(1)} %select_convert_fusion.12), channel_id=1, source_target_pairs={{0,2},{2,0},{1,3},{3,1},{4,6},{6,4},{5,7},{7,5},{8,10},{10,8},{9,1... | collective-permute-start | bytes 49160 | tf_op jit(solution)/shard_map/ppermute | solution.py:21
  395.5 4.3 %collective-permute-done.32 = bf16[16,512]{1,0:T(8,128)(2,1)S(1)} collective-permute-done((bf16[16,512]{1,0:T(8,128)(2,1)S(1)}, bf16[16,512]{1,0:T(8,128)(2,1)S(1)}, u32[]{:S(2)}, u32[]{:S(2)}) %collective-permute-start.32) | collective-permute-done | bytes 16416 | tf_op jit(solution)/shard_map/ppermute | solution.py:21
  399.8 2.9 collective-permute-start.33
  403.2 3.0 collective-permute-done.33
  (628 shorter events, 92.7 us)
Async XLA Ops:
  0.6 51.3 %collective-permute-start.3 = (s32[256]{0:T(256)}, s32[256]{0:T(256)}, u32[]{:S(2)}, u32[]{:S(2)}) collective-permute-start(s32[256]{0:T(256)} %bitcast.409), channel_id=1, source_target_pairs={{1,0},{2,1},{3,2},{4,3},{5,4},{6,5},{7,6},{8,7},{9,8},{10,9},{11,1... | collective-permute-start | bytes 3080 | tf_op jit(solution)/shard_map/ppermute | solution.py:38
  14.9 38.9 %collective-permute-start.2 = (s32[256]{0:T(256)}, s32[256]{0:T(256)}, u32[]{:S(2)}, u32[]{:S(2)}) collective-permute-start(s32[256]{0:T(256)} %bitcast.410), channel_id=1, source_target_pairs={{0,1},{1,2},{2,3},{3,4},{4,5},{5,6},{6,7},{7,8},{8,9},{9,10},{10,1... | collective-permute-start | bytes 3080 | tf_op jit(solution)/shard_map/ppermute | solution.py:37
  19.1 82.0 %collective-permute-start.1 = (bf16[256,512]{0,1:T(8,128)(2,1)}, bf16[256,512]{0,1:T(8,128)(2,1)}, u32[]{:S(2)}, u32[]{:S(2)}) collective-permute-start(bf16[256,512]{0,1:T(8,128)(2,1)} %pad_maximum_fusion.9), channel_id=1, source_target_pairs={{1,0},{2,1},{3,2},{4,3},{5,4},{6,5},{7,6},{8,7},{9,8},{10,9},{11,1... | collective-permute-start | bytes 786440 | tf_op jit(solution)/shard_map/ppermute | solution.py:38
  28.1 73.0 %collective-permute-start = (bf16[256,512]{0,1:T(8,128)(2,1)}, bf16[256,512]{0,1:T(8,128)(2,1)}, u32[]{:S(2)}, u32[]{:S(2)}) collective-permute-start(bf16[256,512]{0,1:T(8,128)(2,1)} %pad_maximum_fusion.9), channel_id=1, source_target_pairs={{0,1},{1,2},{2,3},{3,4},{4,5},{5,6},{6,7},{7,8},{8,9},{9,10},{10,1... | collective-permute-start | bytes 786440 | tf_op jit(solution)/shard_map/ppermute | solution.py:37
  31.8 14.5 %collective-permute-start.11 = (bf16[8,512]{1,0:T(8,128)(2,1)}, bf16[8,512]{1,0:T(8,128)(2,1)}, u32[]{:S(2)}, u32[]{:S(2)}) collective-permute-start(bf16[8,512]{1,0:T(8,128)(2,1)} %pad_maximum_fusion.28), channel_id=1, source_target_pairs={{0,1},{1,0},{2,3},{3,2},{4,5},{5,4},{6,7},{7,6},{8,9},{9,8},{10,11... | collective-permute-start | bytes 24584 | tf_op jit(solution)/shard_map/ppermute | solution.py:21
  38.8 19.1 %copy-start.117 = (s32[1,256]{1,0:T(1,128)S(1)}, s32[1,256]{1,0:T(1,128)}, u32[]{:S(2)}) copy-start(s32[1,256]{1,0:T(1,128)} %param.66) | copy-start | bytes 3076
  40.6 49.2 %copy-start.75 = (bf16[256,128]{0,1:T(8,128)(2,1)}, bf16[256,128]{0,1:T(8,128)(2,1)S(1)}, u32[]{:S(2)}) copy-start(bf16[256,128]{0,1:T(8,128)(2,1)S(1)} %get-tuple-element.557) | copy-start | bytes 196612
  40.6 49.2 %copy-start.77 = (bf16[256,128]{0,1:T(8,128)(2,1)}, bf16[256,128]{0,1:T(8,128)(2,1)S(1)}, u32[]{:S(2)}) copy-start(bf16[256,128]{0,1:T(8,128)(2,1)S(1)} %get-tuple-element.558) | copy-start | bytes 196612
  46.3 19.3 %collective-permute-start.6 = (bf16[32,512]{1,0:T(8,128)(2,1)S(1)}, bf16[32,512]{1,0:T(8,128)(2,1)S(1)}, u32[]{:S(2)}, u32[]{:S(2)}) collective-permute-start(bf16[32,512]{1,0:T(8,128)(2,1)S(1)} %pad_maximum_fusion.21), channel_id=1, source_target_pairs={{0,1},{1,0},{2,3},{3,2},{4,5},{5,4},{6,7},{7,6},{8,9},{9,8},{10,11... | collective-permute-start | bytes 98312 | tf_op jit(solution)/shard_map/ppermute | solution.py:21
  51.9 86.6 %collective-permute-start.4 = (bf16[256,512]{0,1:T(8,128)(2,1)}, bf16[256,512]{0,1:T(8,128)(2,1)}, u32[]{:S(2)}, u32[]{:S(2)}) collective-permute-start(bf16[256,512]{0,1:T(8,128)(2,1)} %pad_maximum_fusion.10), channel_id=1, source_target_pairs={{0,1},{1,0},{2,3},{3,2},{4,5},{5,4},{6,7},{7,6},{8,9},{9,8},{10,11... | collective-permute-start | bytes 786440 | tf_op jit(solution)/shard_map/ppermute | solution.py:21
  53.8 9.8 %collective-permute-start.12 = (bf16[16,512]{1,0:T(8,128)(2,1)S(1)}, bf16[16,512]{1,0:T(8,128)(2,1)S(1)}, u32[]{:S(2)}, u32[]{:S(2)}) collective-permute-start(bf16[16,512]{1,0:T(8,128)(2,1)S(1)} %maximum_select_fusion.13), channel_id=1, source_target_pairs={{0,2},{2,0},{1,3},{3,1},{4,6},{6,4},{5,7},{7,5},{8,10},{10,8},{9,1... | collective-permute-start | bytes 49160 | tf_op jit(solution)/shard_map/ppermute | solution.py:21
  63.7 7.4 %collective-permute-start.13 = (bf16[32,512]{1,0:T(8,128)(2,1)S(1)}, bf16[32,512]{1,0:T(8,128)(2,1)S(1)}, u32[]{:S(2)}, u32[]{:S(2)}) collective-permute-start(bf16[32,512]{1,0:T(8,128)(2,1)S(1)} %maximum_select_fusion.12), channel_id=1, source_target_pairs={{0,4},{4,0},{1,5},{5,1},{2,6},{6,2},{3,7},{7,3},{8,12},{12,8},{9,1... | collective-permute-start | bytes 98312 | tf_op jit(solution)/shard_map/ppermute | solution.py:21
  65.6 12.3 %collective-permute-start.7 = (bf16[64,512]{1,0:T(8,128)(2,1)S(1)}, bf16[64,512]{1,0:T(8,128)(2,1)S(1)}, u32[]{:S(2)}, u32[]{:S(2)}) collective-permute-start(bf16[64,512]{1,0:T(8,128)(2,1)S(1)} %maximum_select_fusion.10), channel_id=1, source_target_pairs={{0,2},{2,0},{1,3},{3,1},{4,6},{6,4},{5,7},{7,5},{8,10},{10,8},{9,1... | collective-permute-start | bytes 196616 | tf_op jit(solution)/shard_map/ppermute | solution.py:21
  71.1 9.5 %collective-permute-start.14 = (bf16[64,512]{1,0:T(8,128)(2,1)S(1)}, bf16[64,512]{1,0:T(8,128)(2,1)S(1)}, u32[]{:S(2)}, u32[]{:S(2)}) collective-permute-start(bf16[64,512]{1,0:T(8,128)(2,1)S(1)} %maximum_select_fusion.11), channel_id=1, source_target_pairs={{0,8},{8,0},{1,9},{9,1},{2,10},{10,2},{3,11},{11,3},{4,12},{12,4},... | collective-permute-start | bytes 196616 | tf_op jit(solution)/shard_map/ppermute | solution.py:21
  77.9 12.2 %collective-permute-start.8 = (bf16[128,512]{1,0:T(8,128)(2,1)S(1)}, bf16[128,512]{1,0:T(8,128)(2,1)S(1)}, u32[]{:S(2)}, u32[]{:S(2)}) collective-permute-start(bf16[128,512]{1,0:T(8,128)(2,1)S(1)} %maximum_select_fusion.8), channel_id=1, source_target_pairs={{0,4},{4,0},{1,5},{5,1},{2,6},{6,2},{3,7},{7,3},{8,12},{12,8},{9,1... | collective-permute-start | bytes 393224 | tf_op jit(solution)/shard_map/ppermute | solution.py:21
  80.6 12.6 %collective-permute-start.15 = (bf16[128,512]{1,0:T(8,128)(2,1)S(1)}, bf16[128,512]{1,0:T(8,128)(2,1)S(1)}, u32[]{:S(2)}, u32[]{:S(2)}) collective-permute-start(bf16[128,512]{1,0:T(8,128)(2,1)S(1)} %maximum_select_fusion.9), channel_id=1, source_target_pairs={{0,16},{16,0},{1,17},{17,1},{2,18},{18,2},{3,19},{19,3},{4,20},{20... | collective-permute-start | bytes 393224 | tf_op jit(solution)/shard_map/ppermute | solution.py:21
  90.0 19.3 %copy-start.52 = (pred[256,768]{0,1:T(8,128)(4,1)}, pred[256,768]{0,1:T(8,128)(4,1)S(1)}, u32[]{:S(2)}) copy-start(pred[256,768]{0,1:T(8,128)(4,1)S(1)} %get-tuple-element.522) | copy-start | bytes 589828
  90.0 19.3 %copy-start.54 = (pred[256,768]{0,1:T(8,128)(4,1)}, pred[256,768]{0,1:T(8,128)(4,1)S(1)}, u32[]{:S(2)}) copy-start(pred[256,768]{0,1:T(8,128)(4,1)S(1)} %get-tuple-element.523) | copy-start | bytes 589828
  90.0 19.3 %copy-start.56 = (pred[256,768]{0,1:T(8,128)(4,1)}, pred[256,768]{0,1:T(8,128)(4,1)S(1)}, u32[]{:S(2)}) copy-start(pred[256,768]{0,1:T(8,128)(4,1)S(1)} %get-tuple-element.524) | copy-start | bytes 589828
  90.0 19.3 %copy-start.58 = (pred[256,768]{0,1:T(8,128)(4,1)}, pred[256,768]{0,1:T(8,128)(4,1)S(1)}, u32[]{:S(2)}) copy-start(pred[256,768]{0,1:T(8,128)(4,1)S(1)} %get-tuple-element.525) | copy-start | bytes 589828
  90.1 19.3 %copy-start.60 = (pred[256,768]{0,1:T(8,128)(4,1)}, pred[256,768]{0,1:T(8,128)(4,1)S(1)}, u32[]{:S(2)}) copy-start(pred[256,768]{0,1:T(8,128)(4,1)S(1)} %get-tuple-element.526) | copy-start | bytes 589828
  90.1 19.3 %copy-start.62 = (pred[256,768]{0,1:T(8,128)(4,1)}, pred[256,768]{0,1:T(8,128)(4,1)S(1)}, u32[]{:S(2)}) copy-start(pred[256,768]{0,1:T(8,128)(4,1)S(1)} %get-tuple-element.527) | copy-start | bytes 589828
  90.1 19.3 %copy-start.64 = (pred[256,768]{0,1:T(8,128)(4,1)}, pred[256,768]{0,1:T(8,128)(4,1)S(1)}, u32[]{:S(2)}) copy-start(pred[256,768]{0,1:T(8,128)(4,1)S(1)} %get-tuple-element.528) | copy-start | bytes 589828
  90.1 19.3 %copy-start.66 = (pred[256,768]{0,1:T(8,128)(4,1)}, pred[256,768]{0,1:T(8,128)(4,1)S(1)}, u32[]{:S(2)}) copy-start(pred[256,768]{0,1:T(8,128)(4,1)S(1)} %get-tuple-element.529) | copy-start | bytes 589828
  90.1 19.3 %copy-start.68 = (pred[256,768]{0,1:T(8,128)(4,1)}, pred[256,768]{0,1:T(8,128)(4,1)S(1)}, u32[]{:S(2)}) copy-start(pred[256,768]{0,1:T(8,128)(4,1)S(1)} %get-tuple-element.530) | copy-start | bytes 589828
  90.1 19.3 %copy-start.70 = (pred[256,768]{0,1:T(8,128)(4,1)}, pred[256,768]{0,1:T(8,128)(4,1)S(1)}, u32[]{:S(2)}) copy-start(pred[256,768]{0,1:T(8,128)(4,1)S(1)} %get-tuple-element.531) | copy-start | bytes 589828
  90.1 19.3 %copy-start.72 = (pred[256,768]{0,1:T(8,128)(4,1)}, pred[256,768]{0,1:T(8,128)(4,1)S(1)}, u32[]{:S(2)}) copy-start(pred[256,768]{0,1:T(8,128)(4,1)S(1)} %get-tuple-element.532) | copy-start | bytes 589828
  90.2 169.0 %collective-permute-start.9 = (bf16[256,512]{1,0:T(8,128)(2,1)S(1)}, bf16[256,512]{1,0:T(8,128)(2,1)}, u32[]{:S(2)}, u32[]{:S(2)}) collective-permute-start(bf16[256,512]{1,0:T(8,128)(2,1)S(1)} %maximum_select_fusion.6), channel_id=1, source_target_pairs={{0,8},{8,0},{1,9},{9,1},{2,10},{10,2},{3,11},{11,3},{4,12},{12,4},... | collective-permute-start | bytes 786440 | tf_op jit(solution)/shard_map/ppermute | solution.py:21
  93.6 170.7 %collective-permute-start.16 = (bf16[256,512]{1,0:T(8,128)(2,1)S(1)}, bf16[256,512]{1,0:T(8,128)(2,1)}, u32[]{:S(2)}, u32[]{:S(2)}) collective-permute-start(bf16[256,512]{1,0:T(8,128)(2,1)S(1)} %maximum_select_fusion.7), channel_id=1, source_target_pairs={{0,32},{32,0},{1,33},{33,1},{2,34},{34,2},{3,35},{35,3},{4,36},{36... | collective-permute-start | bytes 786440 | tf_op jit(solution)/shard_map/ppermute | solution.py:21
  131.5 139.3 %collective-permute-start.18 = (bf16[256,512]{0,1:T(8,128)(2,1)}, bf16[256,512]{0,1:T(8,128)(2,1)}, u32[]{:S(2)}, u32[]{:S(2)}) collective-permute-start(bf16[256,512]{0,1:T(8,128)(2,1)} %get-tuple-element.449), channel_id=1, source_target_pairs={{1,0},{2,1},{3,2},{4,3},{5,4},{6,5},{7,6},{8,7},{9,8},{10,9},{11,1... | collective-permute-start | bytes 786440 | tf_op jit(solution)/shard_map/ppermute | solution.py:27
  136.6 134.3 %collective-permute-start.19 = (bf16[256,512]{0,1:T(8,128)(2,1)}, bf16[256,512]{0,1:T(8,128)(2,1)}, u32[]{:S(2)}, u32[]{:S(2)}) collective-permute-start(bf16[256,512]{0,1:T(8,128)(2,1)} %get-tuple-element.450), channel_id=1, source_target_pairs={{0,1},{1,2},{2,3},{3,4},{4,5},{5,6},{6,7},{7,8},{8,9},{9,10},{10,1... | collective-permute-start | bytes 786440 | tf_op jit(solution)/shard_map/ppermute | solution.py:27
  139.7 133.0 %collective-permute-start.5 = (bf16[512,512]{0,1:T(8,128)(2,1)S(1)}, bf16[512,512]{0,1:T(8,128)(2,1)}, u32[]{:S(2)}, u32[]{:S(2)}) collective-permute-start(bf16[512,512]{0,1:T(8,128)(2,1)S(1)} %maximum_select_fusion.3), channel_id=1, source_target_pairs={{0,2},{2,0},{1,3},{3,1},{4,6},{6,4},{5,7},{7,5},{8,10},{10,8},{9,1... | collective-permute-start | bytes 1572872 | tf_op jit(solution)/shard_map/ppermute | solution.py:21
  260.3 30.9 %collective-permute-start.10 = (bf16[512,512]{1,0:T(8,128)(2,1)S(1)}, bf16[512,512]{1,0:T(8,128)(2,1)}, u32[]{:S(2)}, u32[]{:S(2)}) collective-permute-start(bf16[512,512]{1,0:T(8,128)(2,1)S(1)} %maximum_select_fusion.4), channel_id=1, source_target_pairs={{0,16},{16,0},{1,17},{17,1},{2,18},{18,2},{3,19},{19,3},{4,20},{20... | collective-permute-start | bytes 1572872 | tf_op jit(solution)/shard_map/ppermute | solution.py:21
  266.3 40.2 %collective-permute-start.17 = (bf16[512,512]{1,0:T(8,128)(2,1)}, bf16[512,512]{1,0:T(8,128)(2,1)}, u32[]{:S(2)}, u32[]{:S(2)}) collective-permute-start(bf16[512,512]{1,0:T(8,128)(2,1)} %maximum_select_fusion.5), channel_id=1, source_target_pairs={{0,64},{64,0},{1,65},{65,1},{2,66},{66,2},{3,67},{67,3},{4,68},{68... | collective-permute-start | bytes 1572872 | tf_op jit(solution)/shard_map/ppermute | solution.py:21
  284.7 55.7 %collective-permute-start.20 = (bf16[512,512]{0,1:T(8,128)(2,1)}, bf16[512,512]{0,1:T(8,128)(2,1)}, u32[]{:S(2)}, u32[]{:S(2)}) collective-permute-start(bf16[512,512]{0,1:T(8,128)(2,1)} %select_convert_fusion.2), channel_id=1, source_target_pairs={{0,2},{2,0},{1,3},{3,1},{4,6},{6,4},{5,7},{7,5},{8,10},{10,8},{9,1... | collective-permute-start | bytes 1572872 | tf_op jit(solution)/shard_map/ppermute | solution.py:21
  302.2 42.2 %collective-permute-start.22 = (bf16[512,512]{1,0:T(8,128)(2,1)}, bf16[512,512]{1,0:T(8,128)(2,1)}, u32[]{:S(2)}, u32[]{:S(2)}) collective-permute-start(bf16[512,512]{1,0:T(8,128)(2,1)} %select_convert_fusion.1), channel_id=1, source_target_pairs={{0,16},{16,0},{1,17},{17,1},{2,18},{18,2},{3,19},{19,3},{4,20},{20... | collective-permute-start | bytes 1572872 | tf_op jit(solution)/shard_map/ppermute | solution.py:21
  329.9 18.0 %collective-permute-start.27 = (bf16[512,512]{1,0:T(8,128)(2,1)}, bf16[512,512]{1,0:T(8,128)(2,1)}, u32[]{:S(2)}, u32[]{:S(2)}) collective-permute-start(bf16[512,512]{1,0:T(8,128)(2,1)} %select_convert_fusion), channel_id=1, source_target_pairs={{0,64},{64,0},{1,65},{65,1},{2,66},{66,2},{3,67},{67,3},{4,68},{68... | collective-permute-start | bytes 1572872 | tf_op jit(solution)/shard_map/ppermute | solution.py:21
  342.1 15.1 %collective-permute-start.21 = (bf16[256,512]{0,1:T(8,128)(2,1)S(1)}, bf16[256,512]{0,1:T(8,128)(2,1)S(1)}, u32[]{:S(2)}, u32[]{:S(2)}) collective-permute-start(bf16[256,512]{0,1:T(8,128)(2,1)S(1)} %select_convert_fusion.5), channel_id=1, source_target_pairs={{0,1},{1,0},{2,3},{3,2},{4,5},{5,4},{6,7},{7,6},{8,9},{9,8},{10,11... | collective-permute-start | bytes 786440 | tf_op jit(solution)/shard_map/ppermute | solution.py:21
  345.7 13.5 %collective-permute-start.23 = (bf16[256,512]{1,0:T(8,128)(2,1)S(1)}, bf16[256,512]{1,0:T(8,128)(2,1)S(1)}, u32[]{:S(2)}, u32[]{:S(2)}) collective-permute-start(bf16[256,512]{1,0:T(8,128)(2,1)S(1)} %select_convert_fusion.4), channel_id=1, source_target_pairs={{0,8},{8,0},{1,9},{9,1},{2,10},{10,2},{3,11},{11,3},{4,12},{12,4},... | collective-permute-start | bytes 786440 | tf_op jit(solution)/shard_map/ppermute | solution.py:21
  349.3 12.0 %collective-permute-start.28 = (bf16[256,512]{1,0:T(8,128)(2,1)S(1)}, bf16[256,512]{1,0:T(8,128)(2,1)S(1)}, u32[]{:S(2)}, u32[]{:S(2)}) collective-permute-start(bf16[256,512]{1,0:T(8,128)(2,1)S(1)} %select_convert_fusion.3), channel_id=1, source_target_pairs={{0,32},{32,0},{1,33},{33,1},{2,34},{34,2},{3,35},{35,3},{4,36},{36... | collective-permute-start | bytes 786440 | tf_op jit(solution)/shard_map/ppermute | solution.py:21
  359.4 8.7 %collective-permute-start.24 = (bf16[128,512]{1,0:T(8,128)(2,1)S(1)}, bf16[128,512]{1,0:T(8,128)(2,1)S(1)}, u32[]{:S(2)}, u32[]{:S(2)}) collective-permute-start(bf16[128,512]{1,0:T(8,128)(2,1)S(1)} %select_convert_fusion.7), channel_id=1, source_target_pairs={{0,4},{4,0},{1,5},{5,1},{2,6},{6,2},{3,7},{7,3},{8,12},{12,8},{9,1... | collective-permute-start | bytes 393224 | tf_op jit(solution)/shard_map/ppermute | solution.py:21
  361.5 11.3 %collective-permute-start.29 = (bf16[128,512]{1,0:T(8,128)(2,1)S(1)}, bf16[128,512]{1,0:T(8,128)(2,1)S(1)}, u32[]{:S(2)}, u32[]{:S(2)}) collective-permute-start(bf16[128,512]{1,0:T(8,128)(2,1)S(1)} %select_convert_fusion.6), channel_id=1, source_target_pairs={{0,16},{16,0},{1,17},{17,1},{2,18},{18,2},{3,19},{19,3},{4,20},{20... | collective-permute-start | bytes 393224 | tf_op jit(solution)/shard_map/ppermute | solution.py:21
  368.2 11.5 %collective-permute-start.25 = (bf16[64,512]{1,0:T(8,128)(2,1)S(1)}, bf16[64,512]{1,0:T(8,128)(2,1)S(1)}, u32[]{:S(2)}, u32[]{:S(2)}) collective-permute-start(bf16[64,512]{1,0:T(8,128)(2,1)S(1)} %select_convert_fusion.9), channel_id=1, source_target_pairs={{0,2},{2,0},{1,3},{3,1},{4,6},{6,4},{5,7},{7,5},{8,10},{10,8},{9,1... | collective-permute-start | bytes 196616 | tf_op jit(solution)/shard_map/ppermute | solution.py:21
  372.9 11.4 %collective-permute-start.30 = (bf16[64,512]{1,0:T(8,128)(2,1)S(1)}, bf16[64,512]{1,0:T(8,128)(2,1)S(1)}, u32[]{:S(2)}, u32[]{:S(2)}) collective-permute-start(bf16[64,512]{1,0:T(8,128)(2,1)S(1)} %select_convert_fusion.8), channel_id=1, source_target_pairs={{0,8},{8,0},{1,9},{9,1},{2,10},{10,2},{3,11},{11,3},{4,12},{12,4},... | collective-permute-start | bytes 196616 | tf_op jit(solution)/shard_map/ppermute | solution.py:21
  379.7 7.7 %collective-permute-start.26 = (bf16[32,512]{1,0:T(8,128)(2,1)S(1)}, bf16[32,512]{1,0:T(8,128)(2,1)S(1)}, u32[]{:S(2)}, u32[]{:S(2)}) collective-permute-start(bf16[32,512]{1,0:T(8,128)(2,1)S(1)} %select_convert_fusion.11), channel_id=1, source_target_pairs={{0,1},{1,0},{2,3},{3,2},{4,5},{5,4},{6,7},{7,6},{8,9},{9,8},{10,11... | collective-permute-start | bytes 98312 | tf_op jit(solution)/shard_map/ppermute | solution.py:21
  384.4 5.8 %collective-permute-start.31 = (bf16[32,512]{1,0:T(8,128)(2,1)S(1)}, bf16[32,512]{1,0:T(8,128)(2,1)S(1)}, u32[]{:S(2)}, u32[]{:S(2)}) collective-permute-start(bf16[32,512]{1,0:T(8,128)(2,1)S(1)} %select_convert_fusion.10), channel_id=1, source_target_pairs={{0,4},{4,0},{1,5},{5,1},{2,6},{6,2},{3,7},{7,3},{8,12},{12,8},{9,1... | collective-permute-start | bytes 98312 | tf_op jit(solution)/shard_map/ppermute | solution.py:21
  390.2 9.5 %collective-permute-start.32 = (bf16[16,512]{1,0:T(8,128)(2,1)S(1)}, bf16[16,512]{1,0:T(8,128)(2,1)S(1)}, u32[]{:S(2)}, u32[]{:S(2)}) collective-permute-start(bf16[16,512]{1,0:T(8,128)(2,1)S(1)} %select_convert_fusion.12), channel_id=1, source_target_pairs={{0,2},{2,0},{1,3},{3,1},{4,6},{6,4},{5,7},{7,5},{8,10},{10,8},{9,1... | collective-permute-start | bytes 49160 | tf_op jit(solution)/shard_map/ppermute | solution.py:21
  399.8 6.4 %collective-permute-start.33 = (bf16[8,512]{1,0:T(8,128)(2,1)S(1)}, bf16[8,512]{1,0:T(8,128)(2,1)S(1)}, u32[]{:S(2)}, u32[]{:S(2)}) collective-permute-start(bf16[8,512]{1,0:T(8,128)(2,1)S(1)} %select_convert_fusion.13), channel_id=1, source_target_pairs={{0,1},{1,0},{2,3},{3,2},{4,5},{5,4},{6,7},{7,6},{8,9},{9,8},{10,11... | collective-permute-start | bytes 24584 | tf_op jit(solution)/shard_map/ppermute | solution.py:21
  (170 other events, 1556.4 us)
where the time goes:
time: 416 us; the launch traced here: 409 us
  starting transfers between devices  146 us (35%)
  blocking collectives  112 us (27%)
  other arithmetic  46.6 us (11%)
  local copies, waits for them, and re-layouts  43.8 us (11%)
  matrix products  33 us (8%)
  waiting for transfers between devices  23.4 us (6%)
  between operations  4.5 us (1%)
    ppermute x28, starting transfers between devices, swapped(): return lax.ppermute(block, axis, route)  112 us
    psum x1, blocking collectives, shards(): bias_grad = lax.psum(band[4], ('dp', 'ctx'))  112 us
    ppermute x28, waiting for transfers between devices, swapped(): return lax.ppermute(block, axis, route)  23.4 us
    ppermute x2, starting transfers between devices, with_halo(): after = lax.ppermute(leading, axis, down)  23.3 us
    unnamed x386, local copies, waits for them, and re-layouts  13.6 us
    select_n x14, other arithmetic, double_rows(): jnp.where(upper_half(bit), jnp.concatenate([other, block], axis=0), jnp.c...  10.2 us
    reduce_sum x2, other arithmetic, bucket_sums(): jnp.sum(jnp.where(bucket[None] == level, logit_grads, 0.0), axis=(1, 2))  9.92 us
  transfers between devices with their start and end apart: 34, of which 9 were waited for; matrix products, arithmetic and copies ran while one was open for 29% of the time, Pallas kernels for 0%

commit v1 on v0

--- a/solution.py
+++ b/solution.py
@@ -1,7 +1,7 @@
 import jax
 import jax.numpy as jnp
 from jax import lax
-from jax.sharding import PartitionSpec as P
+from jax.sharding import Mesh, PartitionSpec as P
 
 HEADS = 8
 WINDOW = 512
@@ -9,6 +9,7 @@
 DILATION_FIRST = 1
 DILATION_SECOND = 8
 DILATION_THIRD = 32
+CTX = ("cx", "cy", "cz")
 
 
 def swapped(block, axis, bit):
@@ -57,13 +58,13 @@
 
 
 def upper_half(bit):
-    index = lax.axis_index("ctx")
+    index = lax.axis_index(CTX)
     return index // 2**bit % 2 == 1
 
 
 def double_rows(block, bits):
     for bit in range(bits):
-        other = swapped(block, "ctx", bit)
+        other = swapped(block, CTX, bit)
         block = jnp.where(
             upper_half(bit),
             jnp.concatenate([other, block], axis=0),
@@ -79,7 +80,7 @@
         upper = upper_half(bit)
         outgoing = jnp.where(upper, lower, higher)
         staying = jnp.where(upper, higher, lower)
-        block = staying + swapped(outgoing.astype(jnp.bfloat16), "ctx", bit).astype(outgoing.dtype)
+        block = staying + swapped(outgoing.astype(jnp.bfloat16), CTX, bit).astype(outgoing.dtype)
     return block
 
 
@@ -151,7 +152,7 @@
 
 
 def pass_rim(rim, offset):
-    return shifted(rim.astype(jnp.bfloat16), "ctx", offset).astype(rim.dtype)
+    return shifted(rim.astype(jnp.bfloat16), CTX, offset).astype(rim.dtype)
 
 
 def band_part(query_rows, key_rows, value_rows, grad_rows, clause_rows, table, score_scale):
@@ -161,16 +162,16 @@
     half = WINDOW // 2
     pair_rows = jnp.concatenate([key_rows[:, :wide], value_rows[:, :wide]], axis=1)
     extended, extended_clause = (
-        with_halo(pair_rows, (("ctx", 0),), half),
-        with_halo(clause_rows, (("ctx", 0),), half),
+        with_halo(pair_rows, ((CTX, 0),), half),
+        with_halo(clause_rows, ((CTX, 0),), half),
     )
     reach = rows + 2 * half
     nearby_key_rows = extended[:, :wide].reshape(reach, 2, head_dim)
     values_near = extended[:, wide:].reshape(reach, 2, head_dim)
     query_matrix = query_rows[:, :wide].reshape(rows, 2, head_dim)
     gradient_list = grad_rows[:, :wide].reshape(rows, 2, head_dim)
-    start = lax.axis_index("ctx") * rows
-    length = rows * lax.axis_size("ctx")
+    start = lax.axis_index(CTX) * rows
+    length = rows * lax.axis_size(CTX)
     local_query = jnp.arange(rows)[:, None]
     local_key = jnp.arange(reach)[None, :] - half
     global_key = start + local_key
@@ -211,7 +212,9 @@
     picked_value = sample_rows(value_rows, initial_flag, dilation_rate)
     picked_grad = sample_rows(grad_rows, initial_flag, dilation_rate)
     count = picked_query.shape[0]
-    gathered = span_rows(jnp.concatenate([picked_key, picked_value], axis=1), bits)
+    gathered = lax.all_gather(
+        jnp.concatenate([picked_key, picked_value], axis=1), bits, axis=0, tiled=True
+    )
     gathered_rows = gathered.shape[0]
     every_key_rows = gathered[:, :wide].reshape(gathered_rows, 2, head_dim)
     every_value_rows = gathered[:, wide:].reshape(gathered_rows, 2, head_dim)
@@ -231,7 +234,7 @@
         [key_gradient.reshape(gathered_rows, wide), value_gradient.reshape(gathered_rows, wide)],
         axis=1,
     )
-    own = span_sums(partial_sums, bits)
+    own = lax.psum_scatter(partial_sums, bits, scatter_dimension=0, tiled=True)
     own_key = own[:, :wide].reshape(count, 2, head_dim)
     own_value = own[:, wide:].reshape(count, 2, head_dim)
     return (
@@ -251,15 +254,14 @@
     rows, width = query_rows.shape
     head_dim = width // HEADS
     score_scale = head_dim ** (-0.5)
-    bucket_bit_count = lax.axis_size("ctx").bit_length() - 1
     band = band_part(
         query_rows, key_rows, value_rows, grad_rows, clause_rows, bias_table, score_scale
     )
     pieces = [band[:4]]
     for initial_flag, dilation_rate, bits in (
-        (2, DILATION_FIRST, max(bucket_bit_count - 5, 1)),
-        (4, DILATION_SECOND, bucket_bit_count - 2),
-        (6, DILATION_THIRD, bucket_bit_count),
+        (2, DILATION_FIRST, CTX[2:]),
+        (4, DILATION_SECOND, CTX[1:]),
+        (6, DILATION_THIRD, CTX),
     ):
         pieces.append(
             dilated(
@@ -273,7 +275,7 @@
                 score_scale,
             )
         )
-    bias_grad = lax.psum(band[4], ("dp", "ctx"))
+    bias_grad = lax.psum(band[4], ("dp",) + CTX)
     joined = [
         jnp.concatenate([piece[slot] for piece in pieces], axis=1)
         .reshape(1, rows, width)
@@ -284,19 +286,22 @@
 
 
 def solution(mesh):
+    ctx_size = mesh.shape["ctx"]
+    parts = (4, 8, ctx_size // 32)
+    split = Mesh(mesh.devices.reshape((mesh.shape["dp"],) + parts), ("dp",) + CTX)
     in_specs = (
-        P("dp", "ctx", None),
-        P("dp", "ctx", None),
-        P("dp", "ctx", None),
-        P("dp", "ctx", None),
-        P("dp", "ctx"),
+        P("dp", CTX, None),
+        P("dp", CTX, None),
+        P("dp", CTX, None),
+        P("dp", CTX, None),
+        P("dp", CTX),
         P(),
     )
     out_specs = (
-        P("dp", "ctx", None),
-        P("dp", "ctx", None),
-        P("dp", "ctx", None),
-        P("dp", "ctx", None),
+        P("dp", CTX, None),
+        P("dp", CTX, None),
+        P("dp", CTX, None),
+        P("dp", CTX, None),
         P(),
     )
-    return jax.shard_map(shards, mesh=mesh, in_specs=in_specs, out_specs=out_specs, check_vma=False)
+    return jax.shard_map(shards, mesh=split, in_specs=in_specs, out_specs=out_specs, check_vma=False)

time: 416 us -> 1330 us (3.20)
  the two profiles are of different devices: /device:TPU:6 before, /device:TPU:64 now
where the time goes in v1:
time: 1330 us
  waiting for transfers between devices  1050 us (79%)
  blocking collectives  103 us (8%)
  local copies, waits for them, and re-layouts  80.6 us (6%)
  matrix products  32.6 us (2%)
  other arithmetic  26.9 us (2%)
  starting transfers between devices  24.9 us (2%)
  between operations  16.5 us (1%)
    reduce_scatter x2, waiting for transfers between devices, dilated(): own = lax.psum_scatter(partial_sums, bits, scatter_dimension=0, tiled=True)  796 us
    unnamed x7, waiting for transfers between devices  234 us
    psum x1, blocking collectives, shards(): bias_grad = lax.psum(band[4], ('dp',) + CTX)  103 us
    another operation x33, local copies, waits for them, and re-layouts, bucket_sums(): return jnp.stack(totals, axis=0)  41.6 us
  transfers between devices with their start and end apart: 12, of which 6 were waited for; matrix products, arithmetic and copies ran while one was open for 10% of the time, Pallas kernels for 0%

profile of v1, /device:TPU:64, one launch (start us, length us, event | category | flops | bytes accessed | tf_op | source)
XLA Modules:
  0.0 1330.2 jit_solution(18316485275672854321)
XLA Ops:
  7.2 1.3 copy.505
  8.5 1.3 copy.506
  11.7 1.3 collective-permute-start.3
  13.0 6.7 collective-permute-start.2
  20.5 1.3 collective-permute-start.1
  21.8 7.8 collective-permute-start
  34.0 1.4 fusion.55
  40.6 5.3 fusion.53
  46.3 5.0 collective-permute-done
  53.0 5.7 fusion.9
  60.4 5.5 select_reduce_fusion
  65.9 4.6 all-gather.4.cloned.1.call-done
  71.8 3.7 fusion.132
  75.5 3.2 fusion.60
  78.7 2.3 multiply_reduce_fusion
  83.2 1.5 pad_maximum_fusion
  84.7 5.4 select_reduce_fusion.18
  90.1 1.3 copy.601
  91.5 1.3 copy.602
  92.8 1.3 copy.583
  94.1 1.3 copy.584
  99.1 1.3 copy.597
  100.4 1.3 copy.596
  101.7 1.3 copy.595
  104.3 1.3 copy.593
  108.0 1.3 copy.590
  109.3 1.4 copy.589
  110.6 1.3 copy.588
  116.9 1.3 copy.581
  121.9 1.3 copy.577
  123.2 1.3 copy.576
  125.8 1.3 copy.574
  127.1 1.3 copy.573
  130.9 3.4 fusion.65
  136.6 1.3 collective-permute-start.4
  137.9 6.2 collective-permute-start.5
  145.2 103.3 %psum.7 = f32[32,2]{0,1:T(2,128)} all-reduce(f32[32,2]{0,1:T(2,128)S(1)} %stack.131), channel_id=1, replica_groups=mesh['dp'=4,'cx'=4,'cy'=8,'cz'=4] {'dp','cx','cy','cz'}, use_global_device_ids=true, to_apply=%region_47.48 | all-reduce | flops 64 | bytes 512 | tf_op jit(solution)/shard_map/psum | solution.py:278
  248.4 3.2 fusion.15
  251.6 2.0 fusion.16
  255.7 2.0 convolution_bitcast_fusion
  260.4 1.4 fusion.71
  263.1 1.8 copy.629
  268.9 6.5 all-gather.8.cloned.1.call-done
  278.3 1.3 fusion.77
  281.0 1.9 copy.631
  286.6 38.0 %reduce-scatter.8.cloned.1.call-done = f32[256,512]{0,1:T(8,128)} async-done(((f32[1024,512]{0,1:T(8,128)}), f32[256,512]{0,1:T(8,128)}) %reduce-scatter.8.cloned.1.call-update) | async-done | bytes 524304 | tf_op jit(solution)/shard_map/reduce_scatter | solution.py:237
  327.1 233.6 %reduce-scatter.10.cloned.1.call-done = f32[32,512]{1,0:T(8,128)} async-done(((f32[1024,512]{1,0:T(8,128)}), f32[32,512]{1,0:T(8,128)}) %reduce-scatter.10.cloned.1.call-update) | async-done | bytes 65552
  562.5 757.5 %reduce-scatter.12.cloned.1.call-done = f32[8,512]{1,0:T(8,128)} async-done(((f32[1024,512]{1,0:T(8,128)}), f32[8,512]{1,0:T(8,128)}) %reduce-scatter.12.cloned.1.call-update) | async-done | bytes 16400 | tf_op jit(solution)/shard_map/reduce_scatter | solution.py:237
  (433 shorter events, 66.3 us)
Async XLA Ops:
  7.2 63.3 %all-gather.4.cloned.1.call-start = ((), (), s32[]{:S(2)}) async-start(), calls=%async_computation.3 | async-start | bytes 1310720 | tf_op jit(solution)/shard_map/all_gather | solution.py:215
  10.6 247.0 %all-gather.6.cloned.1.call-start = ((), (), s32[]{:S(2)}) async-start(), calls=%async_computation.4 | async-start | bytes 1081344 | tf_op jit(solution)/shard_map/all_gather | solution.py:215
  10.7 19.7 %copy-start.16 = (f32[32,2]{0,1:T(2,128)S(1)}, f32[32,2]{0,1:T(2,128)}, u32[]{:S(2)}) copy-start(f32[32,2]{0,1:T(2,128)} %param.67) | copy-start | bytes 772
  10.8 20.6 %copy-start.9 = (bf16[1,256,1024]{2,1,0:T(8,128)(2,1)S(1)}, bf16[1,256,1024]{2,1,0:T(8,128)(2,1)}, u32[]{:S(2)}) copy-start(bf16[1,256,1024]{2,1,0:T(8,128)(2,1)} %param.65) | copy-start | bytes 1572868
  11.7 263.7 %all-gather.8.cloned.1.call-start = ((), (), s32[]{:S(2)}) async-start(), calls=%async_computation.5 | async-start | bytes 1056768 | tf_op jit(solution)/shard_map/all_gather | solution.py:215
  11.7 28.8 %collective-permute-start.3 = (s32[256]{0:T(256)S(1)}, s32[256]{0:T(256)S(1)}, u32[]{:S(2)}, u32[]{:S(2)}) collective-permute-start(s32[256]{0:T(256)S(1)} %bitcast.406), channel_id=1, source_target_pairs={{1,0},{2,1},{3,2},{4,3},{5,4},{6,5},{7,6},{8,7},{9,8},{10,9},{11,1... | collective-permute-start | bytes 3080 | tf_op jit(solution)/shard_map/ppermute | solution.py:39
  13.0 27.6 %collective-permute-start.2 = (s32[256]{0:T(256)S(1)}, s32[256]{0:T(256)S(1)}, u32[]{:S(2)}, u32[]{:S(2)}) collective-permute-start(s32[256]{0:T(256)S(1)} %bitcast.407), channel_id=1, source_target_pairs={{0,1},{1,2},{2,3},{3,4},{4,5},{5,6},{6,7},{7,8},{8,9},{9,10},{10,1... | collective-permute-start | bytes 3080 | tf_op jit(solution)/shard_map/ppermute | solution.py:38
  19.8 12.0 copy-start.10
  20.5 25.8 %collective-permute-start.1 = (bf16[256,512]{0,1:T(8,128)(2,1)}, bf16[256,512]{0,1:T(8,128)(2,1)}, u32[]{:S(2)}, u32[]{:S(2)}) collective-permute-start(bf16[256,512]{0,1:T(8,128)(2,1)} %pad_maximum_fusion.9), channel_id=1, source_target_pairs={{1,0},{2,1},{3,2},{4,3},{5,4},{6,5},{7,6},{8,7},{9,8},{10,9},{11,1... | collective-permute-start | bytes 786440 | tf_op jit(solution)/shard_map/ppermute | solution.py:39
  21.8 29.5 %collective-permute-start = (bf16[256,512]{0,1:T(8,128)(2,1)}, bf16[256,512]{0,1:T(8,128)(2,1)}, u32[]{:S(2)}, u32[]{:S(2)}) collective-permute-start(bf16[256,512]{0,1:T(8,128)(2,1)} %pad_maximum_fusion.9), channel_id=1, source_target_pairs={{0,1},{1,2},{2,3},{3,4},{4,5},{5,6},{6,7},{7,8},{8,9},{9,10},{10,1... | collective-permute-start | bytes 786440 | tf_op jit(solution)/shard_map/ppermute | solution.py:38
  30.3 294.3 %reduce-scatter.8.cloned.1.call-start = ((), (), s32[]{:S(2)}) async-start(), calls=%async_computation.6 | async-start | bytes 2621440 | tf_op jit(solution)/shard_map/reduce_scatter | solution.py:237
  84.7 476.0 %reduce-scatter.10.cloned.1.call-start = ((), (), s32[]{:S(2)}) async-start(), calls=%async_computation.7 | async-start | bytes 2162688
  135.4 8.7 copy-start.62
  135.4 8.7 copy-start.63
  135.4 8.7 copy-start.64
  135.4 8.7 copy-start.65
  135.4 8.7 copy-start.66
  135.5 8.7 copy-start.67
  135.5 8.7 copy-start.68
  135.5 8.7 copy-start.69
  135.5 8.7 copy-start.70
  135.5 8.7 copy-start.71
  135.5 8.7 copy-start.72
  135.5 8.7 copy-start.73
  135.5 8.7 copy-start.74
  135.5 8.7 copy-start.75
  135.5 8.7 copy-start.76
  135.6 8.7 copy-start.77
  135.6 8.7 copy-start.78
  135.6 8.7 copy-start.79
  135.6 8.7 copy-start.80
  135.6 8.7 copy-start.81
  135.6 8.7 copy-start.82
  135.6 8.7 copy-start.83
  135.6 8.7 copy-start.84
  135.6 8.7 copy-start.85
  135.6 8.7 copy-start.86
  135.7 8.7 copy-start.87
  135.7 8.7 copy-start.88
  135.7 8.7 copy-start.89
  135.7 8.7 copy-start.90
  135.7 8.7 copy-start.91
  135.7 112.7 %copy-start.58 = (f32[2,256]{1,0:T(2,128)S(1)}, f32[2,256]{1,0:T(2,128)}, u32[]{:S(2)}) copy-start(f32[2,256]{1,0:T(2,128)} %copy-done.57) | copy-start | bytes 6148
  136.6 117.0 %collective-permute-start.4 = (bf16[256,512]{0,1:T(8,128)(2,1)}, bf16[256,512]{0,1:T(8,128)(2,1)}, u32[]{:S(2)}, u32[]{:S(2)}) collective-permute-start(bf16[256,512]{0,1:T(8,128)(2,1)} %get-tuple-element.444), channel_id=1, source_target_pairs={{1,0},{2,1},{3,2},{4,3},{5,4},{6,5},{7,6},{8,7},{9,8},{10,9},{11,1... | collective-permute-start | bytes 786440 | tf_op jit(solution)/shard_map/ppermute | solution.py:28
  137.9 115.7 %collective-permute-start.5 = (bf16[256,512]{0,1:T(8,128)(2,1)}, bf16[256,512]{0,1:T(8,128)(2,1)}, u32[]{:S(2)}, u32[]{:S(2)}) collective-permute-start(bf16[256,512]{0,1:T(8,128)(2,1)} %get-tuple-element.445), channel_id=1, source_target_pairs={{0,1},{1,2},{2,3},{3,4},{4,5},{5,6},{6,7},{7,8},{8,9},{9,10},{10,1... | collective-permute-start | bytes 786440 | tf_op jit(solution)/shard_map/ppermute | solution.py:28
  265.0 1055.0 %reduce-scatter.12.cloned.1.call-start = ((), (), s32[]{:S(2)}) async-start(), calls=%async_computation.8 | async-start | bytes 2113536 | tf_op jit(solution)/shard_map/reduce_scatter | solution.py:237
  267.5 9.2 copy-start.33
  561.8 759.4 %copy-start.38 = (bf16[256,256]{0,1:T(8,128)(2,1)S(1)}, bf16[256,256]{0,1:T(8,128)(2,1)}, u32[]{:S(2)}) copy-start(bf16[256,256]{0,1:T(8,128)(2,1)} %get-tuple-element.482) | copy-start | bytes 393220
  (88 other events, 384.2 us)
Sparse Core Ops, SparseCore 0:
  10.7 59.6 all-gather.3
  73.6 80.2 all-gather.5
  158.3 117.0 all-gather.7
  278.1 46.4 reduce-scatter.7
  329.6 231.0 reduce-scatter.9
  563.3 756.6 reduce-scatter.11
